TPU v7x, 32 devices: a whole 2x2x4 slice. The times are simulated.
32 devices in a mesh: dp: 2 (over x), mp: 16 (over z, y, core).
Axes of the slice: x: 2, y: 2, z: 4, core: 2. Of those that a mesh axis runs over, the one named last changes fastest.
Arguments:
- node_features: bfloat16 [512, 6144], P('mp', 'dp'), may hold values from -6 to 6
- weights_one: bfloat16 [1024, 512], replicated, may hold values from -0.25 to 0.25
- weights_two: bfloat16 [1024, 512], replicated, may hold values from -0.25 to 0.25
- neighbor_owner: int32 [6144, 8], P('dp'), may hold values from 0 to 15, all different within a row; in each aligned block of 192 rows (0 to 191, 192 to 383, ...) at most 144 rows name the same one
- neighbor_row: int32 [6144, 8], P('dp'), may hold values from 0 to 191
- neighbor_count: int32 [6144], P('dp'), may hold values from 4 to 8
- cotangent: bfloat16 [6144, 512], P(('dp', 'mp')), may hold values from -0.076171875 to 0.076171875
Outputs:
- node_output: bfloat16 [6144, 512], P(('dp', 'mp'))
- weight_grads: float32 [2048, 512], P(('dp', 'mp'))
Inputs may be any that keep to these rules, and one draw needn't show every extreme that they name: `neighbor_owner`: each row names 8 different owners; among the rows of one device (aligned blocks of 192 rows) no owner is named more than 144 times, and in some block one owner exactly 144 times. Slots k >= neighbor_count[r] are padding and carry no edge.
All inputs are finite; a program needn't handle non-finite values.
Results may differ from a plain program's by a relative error of at most 0.0052.
Values may be sent and summed in bfloat16 or wider, within the bound.
No kernel may reach another device: no remote copies, remote signals or barrier semaphores. Data moves between devices by JAX's collectives and lax.ppermute only.
A program may use at most 64 MiB of HBM per device.

v0:
```python
import jax
import jax.numpy as jnp
from jax import lax
from jax.sharding import PartitionSpec as P


def column_mean(table, indices, live, inverse):
    total = jnp.zeros((table.shape[0], indices.shape[1]), jnp.float32)
    for slot_index in range(indices.shape[0]):
        picked = jnp.take(table, indices[slot_index], axis=1)
        kept = jnp.where(live[slot_index][None, :], picked, jnp.zeros_like(picked))
        total = total + kept.astype(jnp.float32)
    return (total * inverse[None, :]).astype(jnp.bfloat16)


def silu_slope(values):
    sigmoid = jax.nn.sigmoid(values)
    return sigmoid * (1.0 + values * (1.0 - sigmoid))


def contract(left, right, left_dim, right_dim):
    return lax.dot_general(
        left, right, (((left_dim,), (right_dim,)), ((), ())), preferred_element_type=jnp.float32
    )


def shards(
    node_features, weights_one, weights_two, neighbor_owner, neighbor_row, neighbor_count, cotangent
):
    devices = lax.axis_size("mp")
    own_index = lax.axis_index("mp")
    node_dev = cotangent.shape[0]
    all_nodes = neighbor_owner.shape[0]
    fanout = neighbor_owner.shape[1]
    feat_width = weights_one.shape[0] // 2
    hidden = weights_one.shape[1]
    capacity = 3 * node_dev * fanout // (2 * devices)
    live = lax.broadcasted_iota(jnp.int32, (all_nodes, fanout), 1) < neighbor_count[:, None]
    inverse_all = 1.0 / neighbor_count.astype(jnp.float32)
    owner_ids = lax.broadcasted_iota(jnp.int32, (devices, 1, 1), 0)
    match = (neighbor_owner[None, :, :] == owner_ids) & live[None, :, :]
    rowsel = jnp.max(jnp.where(match, neighbor_row[None, :, :], -1), axis=2)
    has = rowsel >= 0
    with jax.named_scope("layer_one_mean"):
        if all_nodes * all_nodes <= 4096 * 4096:
            row_ids = lax.broadcasted_iota(jnp.int32, (1, node_dev, 1), 1)
            adjacency = (rowsel[:, None, :] == row_ids).astype(jnp.bfloat16)
            adjacency = adjacency.reshape(devices * node_dev, all_nodes)
            summed = contract(node_features, adjacency, 1, 0)
            agg_one_cols = (summed * inverse_all[None, :]).astype(jnp.bfloat16)
        else:
            owner_slots = neighbor_owner.T
            global_ids = owner_slots * node_dev + neighbor_row.T
            agg_one_cols = column_mean(node_features, global_ids, live.T, inverse_all)
    own_feats, own_agg_one = (
        lax.all_to_all(node_features, "mp", split_axis=1, concat_axis=0, tiled=True),
        lax.all_to_all(agg_one_cols, "mp", split_axis=1, concat_axis=0, tiled=True),
    )
    pre_one = contract(weights_one[:feat_width], own_feats, 0, 0) + contract(
        weights_one[feat_width:], own_agg_one, 0, 0
    )
    hidden_one = jax.nn.silu(pre_one).astype(jnp.bfloat16)
    with jax.named_scope("slot_tables"):
        blocks = has.reshape(devices * devices, node_dev).astype(jnp.bfloat16)
        before = (
            lax.broadcasted_iota(jnp.int32, (node_dev, node_dev), 0)
            < lax.broadcasted_iota(jnp.int32, (node_dev, node_dev), 1)
        ).astype(jnp.bfloat16)
        ranks = contract(blocks, before, 1, 0).astype(jnp.int32).reshape(devices, devices, node_dev)
        has_blocks = has.reshape(devices, devices, node_dev)
        rows_blocks = rowsel.reshape(devices, devices, node_dev)
        cap_ids = lax.broadcasted_iota(jnp.int32, (1, capacity, 1), 1)
        own_rank = lax.dynamic_index_in_dim(ranks, own_index, 1, keepdims=False)
        own_has = lax.dynamic_index_in_dim(has_blocks, own_index, 1, keepdims=False)
        gathered = ((own_rank[:, None, :] == cap_ids) & own_has[:, None, :]).astype(jnp.bfloat16)
        gathered = gathered.reshape(devices * capacity, node_dev)
        req_rank = lax.dynamic_index_in_dim(ranks, own_index, 0, keepdims=False)
        req_has = lax.dynamic_index_in_dim(has_blocks, own_index, 0, keepdims=False)
        req_rows = lax.dynamic_index_in_dim(rows_blocks, own_index, 0, keepdims=False)
        pick = ((req_rank[:, None, :] == cap_ids) & req_has[:, None, :]).astype(jnp.bfloat16)
        row_ids = lax.broadcasted_iota(jnp.int32, (1, 1, node_dev), 2)
        which = (req_rows[:, :, None] == row_ids).astype(jnp.bfloat16)
        asked = lax.dot_general(
            pick, which, (((2,), (1,)), ((0,), (0,))), preferred_element_type=jnp.float32
        )
        asked = asked.astype(jnp.bfloat16).reshape(devices * capacity, node_dev)
    own_inverse = lax.dynamic_slice_in_dim(inverse_all, own_index * node_dev, node_dev, 0)
    outgoing = contract(hidden_one, asked, 1, 1).astype(jnp.bfloat16)
    incoming = lax.all_to_all(outgoing, "mp", split_axis=1, concat_axis=1, tiled=True)
    total = contract(incoming, gathered, 1, 0)
    agg_two = (total * own_inverse[None, :]).astype(jnp.bfloat16)
    self_two = weights_two[:hidden]
    neigh_two = weights_two[hidden:]
    node_output = (
        contract(hidden_one, self_two, 0, 0) + contract(agg_two, neigh_two, 0, 0)
    ).astype(jnp.bfloat16)
    down_self = contract(self_two, cotangent, 1, 1)
    down_neigh = (contract(neigh_two, cotangent, 1, 1) * own_inverse[None, :]).astype(jnp.bfloat16)
    outgoing_grad = contract(down_neigh, gathered, 1, 1).astype(jnp.bfloat16)
    incoming_grad = lax.all_to_all(outgoing_grad, "mp", split_axis=1, concat_axis=1, tiled=True)
    neighbor_sum = contract(incoming_grad, asked, 1, 0)
    grad_hidden = down_self + neighbor_sum
    grad_pre = (grad_hidden * silu_slope(pre_one)).astype(jnp.bfloat16)
    terms = jnp.concatenate(
        [
            contract(own_feats, grad_pre, 1, 1),
            contract(own_agg_one, grad_pre, 1, 1),
            contract(hidden_one, cotangent, 1, 0),
            contract(agg_two, cotangent, 1, 0),
        ],
        axis=0,
    )
    weight_grads = lax.psum_scatter(terms, ("dp", "mp"), scatter_dimension=0, tiled=True)
    return (node_output, weight_grads)


def solution(mesh):
    in_specs = (
        P("mp", "dp"),
        P(),
        P(),
        P("dp", None),
        P("dp", None),
        P("dp"),
        P(("dp", "mp"), None),
    )
    out_specs = (P(("dp", "mp"), None), P(("dp", "mp"), None))
    return jax.shard_map(shards, mesh=mesh, in_specs=in_specs, out_specs=out_specs, check_vma=False)
```

profile of v0, /device:TPU:0, one launch (start us, length us, event | category | flops | bytes accessed | tf_op | source)
XLA Modules:
  0.0 325.1 jit_solution(16609977738096543799)
XLA Ops:
  7.2 1.3 all_to_all.40
  9.3 7.4 %all-to-all-start = ((bf16[32,16,192]{2,0,1:T(8,128)(2,1)}), bf16[32,16,192]{2,0,1:T(8,128)(2,1)S(1)}, u32[]{:S(2)}, u32[]{:S(2)}) async-start(bf16[32,16,192]{2,0,1:T(8,128)(2,1)} %copy.27), calls=%async_computation | async-start | bytes 524288 | tf_op jit(solution)/shard_map/all_to_all | solution.py:56
  18.2 1.8 select_reduce_fusion
  20.0 9.7 %bitcast_compare_fusion = pred[3072,3072]{1,0:T(32,128)(4,1)} fusion(s32[3072]{0:T(1024)S(1)} %eq.95, s32[16,3072]{1,0:T(8,128)S(1)} %select_reduce_fusion), kind=kLoop, calls=%fused_computation | loop fusion | flops 9437184 | bytes 9646080 | tf_op jit(solution)/shard_map/layer_one_mean/eq | solution.py:47
  29.9 8.5 %fusion.1 = bf16[32,3072]{1,0:T(8,128)(2,1)S(1)} fusion(pred[3072,3072]{1,0:T(32,128)(4,1)} %bitcast_compare_fusion, bf16[32,3072]{1,0:T(8,128)(2,1)S(1)} %copy-done.7, f32[3072]{0:T(1024)S(1)} %convert_divide_fusion), kind=kOutput, calls=%fused_computation.6 | convolution fusion | flops 604176384 | bytes 9842688 | tf_op jit(solution)/shard_map/layer_one_mean/dot_general | solution.py:22
  40.4 6.1 %all-to-all-start.1 = ((bf16[32,16,192]{2,0,1:T(8,128)(2,1)}), bf16[32,16,192]{2,0,1:T(8,128)(2,1)}, u32[]{:S(2)}, u32[]{:S(2)}) async-start(bf16[32,16,192]{2,0,1:T(8,128)(2,1)} %copy.28), calls=%async_computation.1 | async-start | bytes 524288 | tf_op jit(solution)/shard_map/all_to_all | solution.py:57
  47.2 2.2 convolution_convert_fusion
  49.4 2.5 copy.31
  51.9 4.6 %all-to-all-done.1 = bf16[32,16,192]{2,0,1:T(8,128)(2,1)} async-done(((bf16[32,16,192]{2,0,1:T(8,128)(2,1)}), bf16[32,16,192]{2,0,1:T(8,128)(2,1)}, u32[]{:S(2)}, u32[]{:S(2)}) %all-to-all-start.1) | async-done | bytes 196640 | tf_op jit(solution)/shard_map/all_to_all | solution.py:57
  56.5 3.7 %all-to-all-start.3 = ((bf16[512,16,144]{0,2,1:T(8,128)(2,1)}), bf16[512,16,144]{0,2,1:T(8,128)(2,1)S(1)}, u32[]{:S(2)}, u32[]{:S(2)}) async-start(bf16[512,16,144]{0,2,1:T(8,128)(2,1)} %bitcast.16), calls=%async_computation.3 | async-start | bytes 4718592 | tf_op jit(solution)/shard_map/all_to_all | solution.py:100
  61.1 1.3 fusion.11
  62.8 1.3 fusion.18
  64.1 2.4 convolution_convert_fusion.1
  66.5 4.3 %copy.30 = bf16[512,2304]{0,1:T(8,128)(2,1)} copy(bf16[512,2304]{1,0:T(8,128)(2,1)} %convolution_convert_fusion.1) | data formatting | bytes 4718592 | tf_op jit(solution)/shard_map/convert_element_type | solution.py:88
  70.8 35.1 %all-to-all-done.3 = bf16[512,16,144]{0,2,1:T(8,128)(2,1)S(1)} async-done(((bf16[512,16,144]{0,2,1:T(8,128)(2,1)}), bf16[512,16,144]{0,2,1:T(8,128)(2,1)S(1)}, u32[]{:S(2)}, u32[]{:S(2)}) %all-to-all-start.3) | async-done | bytes 2359328 | tf_op jit(solution)/shard_map/all_to_all | solution.py:100
  105.9 12.3 %all-to-all-start.2 = ((bf16[512,16,144]{0,2,1:T(8,128)(2,1)}), bf16[512,16,144]{0,2,1:T(8,128)(2,1)}, u32[]{:S(2)}, u32[]{:S(2)}) async-start(bf16[512,16,144]{0,2,1:T(8,128)(2,1)} %bitcast.12), calls=%async_computation.2 | async-start | bytes 4718592 | tf_op jit(solution)/shard_map/all_to_all | solution.py:89
  118.2 1.4 fusion.42
  119.6 2.0 convolution_bitcast_fusion.1
  122.0 1.2 fusion.43
  123.5 40.4 %all-to-all-done.2 = bf16[512,16,144]{0,2,1:T(8,128)(2,1)} async-done(((bf16[512,16,144]{0,2,1:T(8,128)(2,1)}), bf16[512,16,144]{0,2,1:T(8,128)(2,1)}, u32[]{:S(2)}, u32[]{:S(2)}) %all-to-all-start.2) | async-done | bytes 2359328 | tf_op jit(solution)/shard_map/all_to_all | solution.py:89
  163.9 2.6 fusion.26
  166.9 2.4 pad_maximum_fusion
  169.3 1.2 copy-done.4
  171.7 146.5 %reduce-scatter.2.cloned.1.call-done = f32[64,512]{1,0:T(8,128)} async-done(((f32[2048,512]{1,0:T(8,128)}), f32[64,512]{1,0:T(8,128)}) %reduce-scatter.2.cloned.1.call-update) | async-done | bytes 131088 | tf_op jit(solution)/shard_map/reduce_scatter | solution.py:113
  (49 shorter events, 8.5 us)
Async XLA Ops:
  7.2 40.0 %copy-start = (bf16[192,512]{1,0:T(8,128)(2,1)S(1)}, bf16[192,512]{1,0:T(8,128)(2,1)}, u32[]{:S(2)}) copy-start(bf16[192,512]{1,0:T(8,128)(2,1)} %param.13) | copy-start | bytes 589828
  9.3 31.1 %all-to-all-start = ((bf16[32,16,192]{2,0,1:T(8,128)(2,1)}), bf16[32,16,192]{2,0,1:T(8,128)(2,1)S(1)}, u32[]{:S(2)}, u32[]{:S(2)}) async-start(bf16[32,16,192]{2,0,1:T(8,128)(2,1)} %copy.27), calls=%async_computation | async-start | bytes 524288 | tf_op jit(solution)/shard_map/all_to_all | solution.py:56
  20.0 9.9 %copy-start.7 = (bf16[32,3072]{1,0:T(8,128)(2,1)S(1)}, bf16[32,3072]{1,0:T(8,128)(2,1)}, u32[]{:S(2)}) copy-start(bf16[32,3072]{1,0:T(8,128)(2,1)} %param.7) | copy-start | bytes 589828
  39.0 7.7 %copy-start.1 = (s32[16,16,192]{2,1,0:T(8,128)}, s32[16,16,192]{2,1,0:T(8,128)S(1)}, u32[]{:S(2)}) copy-start(s32[16,16,192]{2,1,0:T(8,128)S(1)} %reduce_max.12) | copy-start | bytes 589828
  40.2 6.4 %copy-start.6 = (s32[256,192]{1,0:T(8,128)}, s32[256,192]{1,0:T(8,128)S(1)}, u32[]{:S(2)}) copy-start(s32[256,192]{1,0:T(8,128)S(1)} %copy.29) | copy-start | bytes 589828
  40.4 16.2 %all-to-all-start.1 = ((bf16[32,16,192]{2,0,1:T(8,128)(2,1)}), bf16[32,16,192]{2,0,1:T(8,128)(2,1)}, u32[]{:S(2)}, u32[]{:S(2)}) async-start(bf16[32,16,192]{2,0,1:T(8,128)(2,1)} %copy.28), calls=%async_computation.1 | async-start | bytes 524288 | tf_op jit(solution)/shard_map/all_to_all | solution.py:57
  56.5 49.3 %all-to-all-start.3 = ((bf16[512,16,144]{0,2,1:T(8,128)(2,1)}), bf16[512,16,144]{0,2,1:T(8,128)(2,1)S(1)}, u32[]{:S(2)}, u32[]{:S(2)}) async-start(bf16[512,16,144]{0,2,1:T(8,128)(2,1)} %bitcast.16), calls=%async_computation.3 | async-start | bytes 4718592 | tf_op jit(solution)/shard_map/all_to_all | solution.py:100
  60.3 2.2 copy-start.2
  62.5 1.7 copy-start.8
  105.9 58.0 %all-to-all-start.2 = ((bf16[512,16,144]{0,2,1:T(8,128)(2,1)}), bf16[512,16,144]{0,2,1:T(8,128)(2,1)}, u32[]{:S(2)}, u32[]{:S(2)}) async-start(bf16[512,16,144]{0,2,1:T(8,128)(2,1)} %bitcast.12), calls=%async_computation.2 | async-start | bytes 4718592 | tf_op jit(solution)/shard_map/all_to_all | solution.py:89
  118.2 200.1 %reduce-scatter.2.cloned.1.call-start = ((), (), s32[]{:S(2)}) async-start(), calls=%async_computation.5 | async-start | bytes 4325376 | tf_op jit(solution)/shard_map/reduce_scatter | solution.py:113
  119.6 2.0 copy-start.3
  163.9 3.0 copy-start.5
  169.3 1.2 copy-start.4
Sparse Core Ops, SparseCore 0:
  169.4 148.7 reduce-scatter.1
where the time goes:
time: 326 us; the launch traced here: 325 us
  waiting for transfers between devices  227 us (70%)
  starting transfers between devices  29.5 us (9%)
  matrix products  25.9 us (8%)
  other arithmetic  15.9 us (5%)
  between operations  14.4 us (4%)
  local copies, waits for them, and re-layouts  12.7 us (4%)
    reduce_scatter x1, waiting for transfers between devices, shards(): lax.psum_scatter(terms, ('dp', 'mp'), scatter_dimension=0, tiled=True)  147 us
    all_to_all x1, waiting for transfers between devices, shards(): lax.all_to_all(outgoing, 'mp', split_axis=1, concat_axis=1, tiled=True)  40.4 us
    all_to_all x1, waiting for transfers between devices, shards(): lax.all_to_all(outgoing_grad, 'mp', split_axis=1, concat_axis=1, tiled=True)  35.1 us
    dot_general x15, matrix products, contract(): lax.dot_general(left, right, (((left_dim,), (right_dim,)), ((), ())), pre...  24.6 us
    all_to_all x1, starting transfers between devices, shards(): lax.all_to_all(outgoing, 'mp', split_axis=1, concat_axis=1, tiled=True)  12.3 us
    eq x1, other arithmetic, shards(): adjacency = (rowsel[:, None, :] == row_ids).astype(jnp.bfloat16)  9.7 us
    all_to_all x1, starting transfers between devices, shards(): lax.all_to_all(node_features, 'mp', split_axis=1, concat_axis=0, tiled=True)  7.39 us
  transfers between devices with their start and end apart: 5, of which 4 were waited for; matrix products, arithmetic and copies ran while one was open for 14% of the time, Pallas kernels for 0%

commit v1 on v0

--- a/solution.py
+++ b/solution.py
@@ -2,6 +2,25 @@
 import jax.numpy as jnp
 from jax import lax
 from jax.sharding import PartitionSpec as P
+
+
+def _pack_stops_all(state):
+    opened, ready = (lax.axis_size("mp"), lax.axis_index("mp"))
+    work_now = list(state.shape)
+    carry_in = state.shape[1] // opened
+    work_now[1] = carry_in
+    mat_out = work_now[0]
+    work_now[0] = mat_out * opened
+    high = jnp.zeros(work_now, state.dtype)
+    for tick in range(opened):
+        part_next = lax.dynamic_slice_in_dim(state, (ready ^ tick) * carry_in, carry_in, axis=1)
+        if tick:
+            block_list = []
+            for num in range(opened):
+                block_list.append((num, num ^ tick))
+            part_next = lax.ppermute(part_next, axis_name="mp", perm=block_list)
+        high = lax.dynamic_update_slice_in_dim(high, part_next, (ready ^ tick) * mat_out, axis=0)
+    return high
 
 
 def column_mean(table, indices, live, inverse):
@@ -54,7 +73,7 @@
             agg_one_cols = column_mean(node_features, global_ids, live.T, inverse_all)
     own_feats, own_agg_one = (
         lax.all_to_all(node_features, "mp", split_axis=1, concat_axis=0, tiled=True),
-        lax.all_to_all(agg_one_cols, "mp", split_axis=1, concat_axis=0, tiled=True),
+        _pack_stops_all(agg_one_cols),
     )
     pre_one = contract(weights_one[:feat_width], own_feats, 0, 0) + contract(
         weights_one[feat_width:], own_agg_one, 0, 0

time: 326 us -> 321 us (0.985)
  waiting for transfers between devices: 227 us -> 209 us
  starting transfers between devices: 29.5 us -> 40.5 us
    all_to_all x1, waiting for transfers between devices: 35.1 us -> 0.01 us  [shards(): lax.all_to_all(outgoing_grad, 'mp', split_axis=1, concat_axis=1, tiled=True)]
    ppermute x0 -> x15, starting transfers between devices: none -> 22.8 us  [_pack_stops_all(): part_next = lax.ppermute(part_next, axis_name='mp', perm=block_list)]
    ppermute x0 -> x15, waiting for transfers between devices: none -> 21.7 us  [_pack_stops_all(): part_next = lax.ppermute(part_next, axis_name='mp', perm=block_list)]
    all_to_all x1, starting transfers between devices: 12.3 us -> 4.45 us  [shards(): lax.all_to_all(outgoing, 'mp', split_axis=1, concat_axis=1, tiled=True)]
    all_to_all x1 -> x0, starting transfers between devices: 6.07 us -> none  [shards(): lax.all_to_all(agg_one_cols, 'mp', split_axis=1, concat_axis=0, tiled=True)]
    all_to_all x1 -> x0, waiting for transfers between devices: 4.64 us -> none  [shards(): lax.all_to_all(agg_one_cols, 'mp', split_axis=1, concat_axis=0, tiled=True)]
  transfers between devices with their start and end apart: 5 -> 19, of which waited for: 4 -> 7; matrix products, arithmetic and copies ran while one was open for 14% -> 15% of each run, Pallas kernels for 0% -> 0%
where the time goes in v1:
time: 321 us; the launch traced here: 320 us
  waiting for transfers between devices  209 us (65%)
  starting transfers between devices  40.5 us (13%)
  matrix products  27.6 us (9%)
  other arithmetic  15.9 us (5%)
  between operations  14.5 us (5%)
  local copies, waits for them, and re-layouts  12.4 us (4%)
    reduce_scatter x1, waiting for transfers between devices, shards(): lax.psum_scatter(terms, ('dp', 'mp'), scatter_dimension=0, tiled=True)  147 us
    all_to_all x1, waiting for transfers between devices, shards(): lax.all_to_all(outgoing, 'mp', split_axis=1, concat_axis=1, tiled=True)  40.3 us
    dot_general x15, matrix products, contract(): lax.dot_general(left, right, (((left_dim,), (right_dim,)), ((), ())), pre...  25.5 us
    ppermute x15, starting transfers between devices, _pack_stops_all(): part_next = lax.ppermute(part_next, axis_name='mp', perm=block_list)  22.8 us
    ppermute x15, waiting for transfers between devices, _pack_stops_all(): part_next = lax.ppermute(part_next, axis_name='mp', perm=block_list)  21.7 us
    eq x1, other arithmetic, shards(): adjacency = (rowsel[:, None, :] == row_ids).astype(jnp.bfloat16)  9.71 us
    all_to_all x1, starting transfers between devices, shards(): lax.all_to_all(node_features, 'mp', split_axis=1, concat_axis=0, tiled=True)  7.44 us
  transfers between devices with their start and end apart: 19, of which 7 were waited for; matrix products, arithmetic and copies ran while one was open for 15% of the time, Pallas kernels for 0%

profile of v1, /device:TPU:0, one launch (start us, length us, event | category | flops | bytes accessed | tf_op | source)
XLA Modules:
  0.0 319.9 jit_solution(17859688942353271511)
XLA Ops:
  9.3 7.4 %all-to-all-start = ((bf16[32,16,192]{2,0,1:T(8,128)(2,1)}), bf16[32,16,192]{2,0,1:T(8,128)(2,1)}, u32[]{:S(2)}, u32[]{:S(2)}) async-start(bf16[32,16,192]{2,0,1:T(8,128)(2,1)} %copy.25), calls=%async_computation | async-start | bytes 524288 | tf_op jit(solution)/shard_map/all_to_all | solution.py:75
  21.8 2.2 convolution_convert_fusion
  24.1 2.5 copy.28
  26.8 5.8 %all-to-all-start.2 = ((bf16[512,16,144]{0,2,1:T(8,128)(2,1)}), bf16[512,16,144]{0,2,1:T(8,128)(2,1)S(1)}, u32[]{:S(2)}, u32[]{:S(2)}) async-start(bf16[512,16,144]{0,2,1:T(8,128)(2,1)} %bitcast.29), calls=%async_computation.2 | async-start | bytes 4718592 | tf_op jit(solution)/shard_map/all_to_all | solution.py:119
  32.7 9.7 %bitcast_compare_fusion = pred[3072,3072]{1,0:T(32,128)(4,1)} fusion(s32[3072]{0:T(1024)S(1)} %eq.95, s32[16,3072]{1,0:T(8,128)S(1)} %select_reduce_fusion), kind=kLoop, calls=%fused_computation | loop fusion | flops 9437184 | bytes 9646080 | tf_op jit(solution)/shard_map/layer_one_mean/eq | solution.py:66
  42.4 8.5 %fusion = bf16[3072,32]{0,1:T(8,128)(2,1)S(1)} fusion(pred[3072,3072]{1,0:T(32,128)(4,1)} %bitcast_compare_fusion, bf16[32,3072]{1,0:T(8,128)(2,1)S(1)} %copy-done.8, f32[3072]{0:T(1024)S(1)} %convert_divide_fusion), kind=kOutput, calls=%fused_computation.5 | convolution fusion | flops 604176384 | bytes 9842688 | tf_op jit(solution)/shard_map/layer_one_mean/dot_general | solution.py:41
  55.9 2.1 fusion.10
  58.1 2.6 collective-permute-start.5
  60.9 2.5 collective-permute-start.7
  63.4 8.8 %collective-permute-done.3 = bf16[32,192]{1,0:T(8,128)(2,1)S(1)} collective-permute-done((bf16[32,192]{1,0:T(8,128)(2,1)S(1)}, bf16[32,192]{1,0:T(8,128)(2,1)S(1)}, u32[]{:S(2)}, u32[]{:S(2)}) %collective-permute-start.3) | collective-permute-done | bytes 12320 | tf_op jit(solution)/shard_map/ppermute | solution.py:21
  72.2 3.5 %collective-permute-start.8 = (bf16[32,192]{1,0:T(8,128)(2,1)S(1)}, bf16[32,192]{1,0:T(8,128)(2,1)S(1)}, u32[]{:S(2)}, u32[]{:S(2)}) collective-permute-start(bf16[32,192]{1,0:T(8,128)(2,1)S(1)} %get-tuple-element.8), channel_id=1, source_target_pairs={{0,9},{1,8},{2,11},{3,10},{4,13},{5,12},{6,15},{7,14},{8,1},{9,0},... | collective-permute-start | bytes 36872 | tf_op jit(solution)/shard_map/ppermute | solution.py:21
  75.7 2.4 collective-permute-start.9
  78.1 2.1 collective-permute-start.10
  80.3 9.5 %collective-permute-done.7 = bf16[32,192]{1,0:T(8,128)(2,1)S(1)} collective-permute-done((bf16[32,192]{1,0:T(8,128)(2,1)S(1)}, bf16[32,192]{1,0:T(8,128)(2,1)S(1)}, u32[]{:S(2)}, u32[]{:S(2)}) %collective-permute-start.7) | collective-permute-done | bytes 12320 | tf_op jit(solution)/shard_map/ppermute | solution.py:21
  89.8 3.2 %collective-permute-start.13 = (bf16[32,192]{1,0:T(8,128)(2,1)S(1)}, bf16[32,192]{1,0:T(8,128)(2,1)S(1)}, u32[]{:S(2)}, u32[]{:S(2)}) collective-permute-start(bf16[32,192]{1,0:T(8,128)(2,1)S(1)} %get-tuple-element.3), channel_id=1, source_target_pairs={{0,14},{1,15},{2,12},{3,13},{4,10},{5,11},{6,8},{7,9},{8,6},{9,7},... | collective-permute-start | bytes 36872 | tf_op jit(solution)/shard_map/ppermute | solution.py:21
  93.1 2.4 collective-permute-start.14
  96.3 2.6 collective-permute-done.14
  101.7 2.4 convolution_convert_fusion.1
  104.1 4.3 %copy.27 = bf16[512,2304]{0,1:T(8,128)(2,1)} copy(bf16[512,2304]{1,0:T(8,128)(2,1)} %convolution_convert_fusion.1) | data formatting | bytes 4718592 | tf_op jit(solution)/shard_map/convert_element_type | solution.py:107
  108.4 4.4 %all-to-all-start.1 = ((bf16[512,16,144]{0,2,1:T(8,128)(2,1)}), bf16[512,16,144]{0,2,1:T(8,128)(2,1)}, u32[]{:S(2)}, u32[]{:S(2)}) async-start(bf16[512,16,144]{0,2,1:T(8,128)(2,1)} %bitcast.25), calls=%async_computation.1 | async-start | bytes 4718592 | tf_op jit(solution)/shard_map/all_to_all | solution.py:108
  118.2 40.3 %all-to-all-done.1 = bf16[512,16,144]{0,2,1:T(8,128)(2,1)} async-done(((bf16[512,16,144]{0,2,1:T(8,128)(2,1)}), bf16[512,16,144]{0,2,1:T(8,128)(2,1)}, u32[]{:S(2)}, u32[]{:S(2)}) %all-to-all-start.1) | async-done | bytes 2359328 | tf_op jit(solution)/shard_map/all_to_all | solution.py:108
  158.5 2.5 fusion.25
  161.4 2.4 pad_maximum_fusion
  166.4 146.6 %reduce-scatter.2.cloned.1.call-done = f32[64,512]{1,0:T(8,128)} async-done(((f32[2048,512]{1,0:T(8,128)}), f32[64,512]{1,0:T(8,128)}) %reduce-scatter.2.cloned.1.call-update) | async-done | bytes 131088 | tf_op jit(solution)/shard_map/reduce_scatter | solution.py:132
  (99 shorter events, 24.3 us)
Async XLA Ops:
  7.2 14.7 %copy-start = (bf16[192,512]{1,0:T(8,128)(2,1)S(1)}, bf16[192,512]{1,0:T(8,128)(2,1)}, u32[]{:S(2)}) copy-start(bf16[192,512]{1,0:T(8,128)(2,1)} %param.13) | copy-start | bytes 589828
  9.3 17.5 %all-to-all-start = ((bf16[32,16,192]{2,0,1:T(8,128)(2,1)}), bf16[32,16,192]{2,0,1:T(8,128)(2,1)}, u32[]{:S(2)}, u32[]{:S(2)}) async-start(bf16[32,16,192]{2,0,1:T(8,128)(2,1)} %copy.25), calls=%async_computation | async-start | bytes 524288 | tf_op jit(solution)/shard_map/all_to_all | solution.py:75
  26.8 81.6 %all-to-all-start.2 = ((bf16[512,16,144]{0,2,1:T(8,128)(2,1)}), bf16[512,16,144]{0,2,1:T(8,128)(2,1)S(1)}, u32[]{:S(2)}, u32[]{:S(2)}) async-start(bf16[512,16,144]{0,2,1:T(8,128)(2,1)} %bitcast.29), calls=%async_computation.2 | async-start | bytes 4718592 | tf_op jit(solution)/shard_map/all_to_all | solution.py:119
  32.7 9.7 %copy-start.8 = (bf16[32,3072]{1,0:T(8,128)(2,1)S(1)}, bf16[32,3072]{1,0:T(8,128)(2,1)}, u32[]{:S(2)}) copy-start(bf16[32,3072]{1,0:T(8,128)(2,1)} %param.7) | copy-start | bytes 589828
  51.2 6.9 %collective-permute-start = (bf16[32,192]{1,0:T(8,128)(2,1)S(1)}, bf16[32,192]{1,0:T(8,128)(2,1)S(1)}, u32[]{:S(2)}, u32[]{:S(2)}) collective-permute-start(bf16[32,192]{1,0:T(8,128)(2,1)S(1)} %get-tuple-element.16), channel_id=1, source_target_pairs={{0,1},{1,0},{2,3},{3,2},{4,5},{5,4},{6,7},{7,6},{8,9},{9,8},{10,11... | collective-permute-start | bytes 36872 | tf_op jit(solution)/shard_map/ppermute | solution.py:21
  51.6 9.2 %collective-permute-start.1 = (bf16[32,192]{1,0:T(8,128)(2,1)S(1)}, bf16[32,192]{1,0:T(8,128)(2,1)S(1)}, u32[]{:S(2)}, u32[]{:S(2)}) collective-permute-start(bf16[32,192]{1,0:T(8,128)(2,1)S(1)} %get-tuple-element.15), channel_id=1, source_target_pairs={{0,2},{1,3},{2,0},{3,1},{4,6},{5,7},{6,4},{7,5},{8,10},{9,11},{10,... | collective-permute-start | bytes 36872 | tf_op jit(solution)/shard_map/ppermute | solution.py:21
  53.3 7.6 %collective-permute-start.2 = (bf16[32,192]{1,0:T(8,128)(2,1)S(1)}, bf16[32,192]{1,0:T(8,128)(2,1)S(1)}, u32[]{:S(2)}, u32[]{:S(2)}) collective-permute-start(bf16[32,192]{1,0:T(8,128)(2,1)S(1)} %get-tuple-element.14), channel_id=1, source_target_pairs={{0,3},{1,2},{2,1},{3,0},{4,7},{5,6},{6,5},{7,4},{8,11},{9,10},{10,... | collective-permute-start | bytes 36872 | tf_op jit(solution)/shard_map/ppermute | solution.py:21
  53.3 18.9 %collective-permute-start.3 = (bf16[32,192]{1,0:T(8,128)(2,1)S(1)}, bf16[32,192]{1,0:T(8,128)(2,1)S(1)}, u32[]{:S(2)}, u32[]{:S(2)}) collective-permute-start(bf16[32,192]{1,0:T(8,128)(2,1)S(1)} %get-tuple-element.13), channel_id=1, source_target_pairs={{0,4},{1,5},{2,6},{3,7},{4,0},{5,1},{6,2},{7,3},{8,12},{9,13},{10,... | collective-permute-start | bytes 36872 | tf_op jit(solution)/shard_map/ppermute | solution.py:21
  55.0 20.7 %collective-permute-start.4 = (bf16[32,192]{1,0:T(8,128)(2,1)S(1)}, bf16[32,192]{1,0:T(8,128)(2,1)S(1)}, u32[]{:S(2)}, u32[]{:S(2)}) collective-permute-start(bf16[32,192]{1,0:T(8,128)(2,1)S(1)} %get-tuple-element.12), channel_id=1, source_target_pairs={{0,5},{1,4},{2,7},{3,6},{4,1},{5,0},{6,3},{7,2},{8,13},{9,12},{10,... | collective-permute-start | bytes 36872 | tf_op jit(solution)/shard_map/ppermute | solution.py:21
  58.1 43.6 %copy-start.11 = (bf16[16,144,192]{2,1,0:T(8,128)(2,1)S(1)}, bf16[16,144,192]{2,1,0:T(8,128)(2,1)}, u32[]{:S(2)}) copy-start(bf16[16,144,192]{2,1,0:T(8,128)(2,1)} %fusion.10) | copy-start | bytes 2654212
  58.1 19.9 %collective-permute-start.5 = (bf16[32,192]{1,0:T(8,128)(2,1)S(1)}, bf16[32,192]{1,0:T(8,128)(2,1)S(1)}, u32[]{:S(2)}, u32[]{:S(2)}) collective-permute-start(bf16[32,192]{1,0:T(8,128)(2,1)S(1)} %get-tuple-element.11), channel_id=1, source_target_pairs={{0,6},{1,7},{2,4},{3,5},{4,2},{5,3},{6,0},{7,1},{8,14},{9,15},{10,... | collective-permute-start | bytes 36872 | tf_op jit(solution)/shard_map/ppermute | solution.py:21
  60.8 19.4 %collective-permute-start.6 = (bf16[32,192]{1,0:T(8,128)(2,1)S(1)}, bf16[32,192]{1,0:T(8,128)(2,1)S(1)}, u32[]{:S(2)}, u32[]{:S(2)}) collective-permute-start(bf16[32,192]{1,0:T(8,128)(2,1)S(1)} %get-tuple-element.10), channel_id=1, source_target_pairs={{0,7},{1,6},{2,5},{3,4},{4,3},{5,2},{6,1},{7,0},{8,15},{9,14},{10,... | collective-permute-start | bytes 36872 | tf_op jit(solution)/shard_map/ppermute | solution.py:21
  60.9 29.0 %collective-permute-start.7 = (bf16[32,192]{1,0:T(8,128)(2,1)S(1)}, bf16[32,192]{1,0:T(8,128)(2,1)S(1)}, u32[]{:S(2)}, u32[]{:S(2)}) collective-permute-start(bf16[32,192]{1,0:T(8,128)(2,1)S(1)} %get-tuple-element.9), channel_id=1, source_target_pairs={{0,8},{1,9},{2,10},{3,11},{4,12},{5,13},{6,14},{7,15},{8,0},{9,1},... | collective-permute-start | bytes 36872 | tf_op jit(solution)/shard_map/ppermute | solution.py:21
  72.2 17.6 %collective-permute-start.8 = (bf16[32,192]{1,0:T(8,128)(2,1)S(1)}, bf16[32,192]{1,0:T(8,128)(2,1)S(1)}, u32[]{:S(2)}, u32[]{:S(2)}) collective-permute-start(bf16[32,192]{1,0:T(8,128)(2,1)S(1)} %get-tuple-element.8), channel_id=1, source_target_pairs={{0,9},{1,8},{2,11},{3,10},{4,13},{5,12},{6,15},{7,14},{8,1},{9,0},... | collective-permute-start | bytes 36872 | tf_op jit(solution)/shard_map/ppermute | solution.py:21
  75.7 17.4 %collective-permute-start.9 = (bf16[32,192]{1,0:T(8,128)(2,1)S(1)}, bf16[32,192]{1,0:T(8,128)(2,1)S(1)}, u32[]{:S(2)}, u32[]{:S(2)}) collective-permute-start(bf16[32,192]{1,0:T(8,128)(2,1)S(1)} %get-tuple-element.7), channel_id=1, source_target_pairs={{0,10},{1,11},{2,8},{3,9},{4,14},{5,15},{6,12},{7,13},{8,2},{9,3},... | collective-permute-start | bytes 36872 | tf_op jit(solution)/shard_map/ppermute | solution.py:21
  78.1 17.4 %collective-permute-start.10 = (bf16[32,192]{1,0:T(8,128)(2,1)S(1)}, bf16[32,192]{1,0:T(8,128)(2,1)S(1)}, u32[]{:S(2)}, u32[]{:S(2)}) collective-permute-start(bf16[32,192]{1,0:T(8,128)(2,1)S(1)} %get-tuple-element.6), channel_id=1, source_target_pairs={{0,11},{1,10},{2,9},{3,8},{4,15},{5,14},{6,13},{7,12},{8,3},{9,2},... | collective-permute-start | bytes 36872 | tf_op jit(solution)/shard_map/ppermute | solution.py:21
  80.2 15.2 %collective-permute-start.11 = (bf16[32,192]{1,0:T(8,128)(2,1)S(1)}, bf16[32,192]{1,0:T(8,128)(2,1)S(1)}, u32[]{:S(2)}, u32[]{:S(2)}) collective-permute-start(bf16[32,192]{1,0:T(8,128)(2,1)S(1)} %get-tuple-element.5), channel_id=1, source_target_pairs={{0,12},{1,13},{2,14},{3,15},{4,8},{5,9},{6,10},{7,11},{8,4},{9,5},... | collective-permute-start | bytes 36872 | tf_op jit(solution)/shard_map/ppermute | solution.py:21
  89.8 5.7 %collective-permute-start.12 = (bf16[32,192]{1,0:T(8,128)(2,1)S(1)}, bf16[32,192]{1,0:T(8,128)(2,1)S(1)}, u32[]{:S(2)}, u32[]{:S(2)}) collective-permute-start(bf16[32,192]{1,0:T(8,128)(2,1)S(1)} %get-tuple-element.4), channel_id=1, source_target_pairs={{0,13},{1,12},{2,15},{3,14},{4,9},{5,8},{6,11},{7,10},{8,5},{9,4},... | collective-permute-start | bytes 36872 | tf_op jit(solution)/shard_map/ppermute | solution.py:21
  89.8 6.5 %collective-permute-start.13 = (bf16[32,192]{1,0:T(8,128)(2,1)S(1)}, bf16[32,192]{1,0:T(8,128)(2,1)S(1)}, u32[]{:S(2)}, u32[]{:S(2)}) collective-permute-start(bf16[32,192]{1,0:T(8,128)(2,1)S(1)} %get-tuple-element.3), channel_id=1, source_target_pairs={{0,14},{1,15},{2,12},{3,13},{4,10},{5,11},{6,8},{7,9},{8,6},{9,7},... | collective-permute-start | bytes 36872 | tf_op jit(solution)/shard_map/ppermute | solution.py:21
  93.1 5.9 %collective-permute-start.14 = (bf16[32,192]{1,0:T(8,128)(2,1)S(1)}, bf16[32,192]{1,0:T(8,128)(2,1)S(1)}, u32[]{:S(2)}, u32[]{:S(2)}) collective-permute-start(bf16[32,192]{1,0:T(8,128)(2,1)S(1)} %get-tuple-element.2), channel_id=1, source_target_pairs={{0,15},{1,14},{2,13},{3,12},{4,11},{5,10},{6,9},{7,8},{8,7},{9,6},... | collective-permute-start | bytes 36872 | tf_op jit(solution)/shard_map/ppermute | solution.py:21
  101.7 14.6 %copy-start.5 = (f32[512,192]{0,1:T(8,128)}, f32[512,192]{0,1:T(8,128)S(1)}, u32[]{:S(2)}) copy-start(f32[512,192]{0,1:T(8,128)S(1)} %fusion.17) | copy-start | bytes 1179652
  108.4 50.1 %all-to-all-start.1 = ((bf16[512,16,144]{0,2,1:T(8,128)(2,1)}), bf16[512,16,144]{0,2,1:T(8,128)(2,1)}, u32[]{:S(2)}, u32[]{:S(2)}) async-start(bf16[512,16,144]{0,2,1:T(8,128)(2,1)} %bitcast.25), calls=%async_computation.1 | async-start | bytes 4718592 | tf_op jit(solution)/shard_map/all_to_all | solution.py:108
  112.9 200.1 %reduce-scatter.2.cloned.1.call-start = ((), (), s32[]{:S(2)}) async-start(), calls=%async_computation.4 | async-start | bytes 4325376 | tf_op jit(solution)/shard_map/reduce_scatter | solution.py:132
  118.2 43.2 %copy-start.4 = (f32[512,512]{1,0:T(8,128)S(1)}, f32[512,512]{1,0:T(8,128)}, u32[]{:S(2)}) copy-start(f32[512,512]{1,0:T(8,128)} %fusion.41) | copy-start | bytes 3145732
  (7 other events, 17.6 us)
Sparse Core Ops, SparseCore 0:
  164.0 148.9 reduce-scatter.1
